TPU v7x, 128 devices: a whole 4x4x4 slice. The times are simulated.
128 devices in a mesh: ctx: 16 (over y_lo, z, core), head: 8 (over x, y_hi).
Axes of the slice: x: 4, y: 4 (y_hi: 2, y_lo: 2; y = y_hi * 2 + y_lo), z: 4, core: 2. Of those that a mesh axis runs over, the one named last changes fastest.
Arguments:
- hidden_in: bfloat16 [4096, 8192], P('ctx', 'head'), may hold values from -90 to 90
- query_rows: bfloat16 [4096, 8192], P('ctx', 'head'), may hold values from -5 to 5
- key_rows: bfloat16 [4096, 1024], P('ctx', 'head'), may hold values from -5 to 5
- value_rows: bfloat16 [4096, 1024], P('ctx', 'head'), may hold values from -6 to 6
- out_weight: bfloat16 [8192, 8192], P('head'), may hold values from -0.0625 to 0.0625
- grad_out: bfloat16 [4096, 8192], P('ctx', 'head'), may hold values from -6 to 6
- answer_mask: int32 [4096], P('ctx'), may hold values 0 or 1
Outputs:
- grad_query: bfloat16 [4096, 8192], P('ctx', 'head')
- grad_key: bfloat16 [4096, 1024], P('ctx', 'head')
- grad_value: bfloat16 [4096, 1024], P('ctx', 'head')
- fisher_q: float32 [16, 64], P('ctx', 'head')
- fisher_o: float32 [16, 64], P('ctx', 'head')
All inputs are finite; a program needn't handle non-finite values. No bound on the sum of `answer_mask` on one device may be relied on, other than what follows from the above.
Results may differ from a plain program's by a relative error of at most 0.019.
Values may be sent and summed in bfloat16 or wider, within the bound.
No kernel may reach another device: no remote copies, remote signals or barrier semaphores. Data moves between devices by JAX's collectives and lax.ppermute only.
A program may use at most 128 MiB of HBM per device.

v0:
```python
import math
import jax
import jax.numpy as jnp
from jax import lax
from jax.sharding import PartitionSpec as P

D = 8192
HEADS = 64
KVH = 8
HD = 128
NEGATIVE = -1e30
EPSILON = 1e-06


def block_scores(query_group, key_block, scaling, row_pos, col_pos):
    scores = (
        jnp.einsum("tgd,kd->tgk", query_group, key_block, preferred_element_type=jnp.float32)
        * scaling
    )
    return jnp.where(row_pos[:, None, None] >= col_pos[None, None, :], scores, NEGATIVE)


def head_squares(left_side, right_side, head_dim):
    product = lax.dot_general(
        left_side, right_side, (((0,), (0,)), ((), ())), preferred_element_type=jnp.float32
    )
    shaped = (product * product).reshape(
        product.shape[0], right_side.shape[1] // head_dim, head_dim
    )
    return jnp.sum(shaped, axis=(0, 2))


def gram_pair_squares(left_gram, right_side, head_dim):
    rows = right_side.shape[0]
    right_heads = right_side.reshape(rows, right_side.shape[1] // head_dim, head_dim)
    right_gram = jnp.einsum(
        "ihd,jhd->hij", right_heads, right_heads, preferred_element_type=jnp.float32
    )
    return jnp.sum(right_gram * left_gram[None], axis=(1, 2))


def gram_squares(left_side, right_side, head_dim):
    left_gram = lax.dot_general(
        left_side, left_side, (((1,), (1,)), ((), ())), preferred_element_type=jnp.float32
    )
    return gram_pair_squares(left_gram, right_side, head_dim)


def body(hidden_in, query_rows, key_rows, value_rows, out_weight, grad_out, answer_mask):
    tok_dev = query_rows.shape[0]
    head_dim = HD
    group_size = HEADS // KVH
    local_groups = key_rows.shape[1] // head_dim
    scaling = head_dim ** (-0.5)
    own_index = lax.axis_index("ctx")
    first_row = own_index * tok_dev
    loss_weight = 0.25 + answer_mask.astype(jnp.float32)
    weighted = (grad_out.astype(jnp.float32) * loss_weight[:, None]).astype(jnp.bfloat16)
    hidden_gram = lax.psum(
        lax.dot_general(
            hidden_in, hidden_in, (((1,), (1,)), ((), ())), preferred_element_type=jnp.float32
        ),
        "head",
    )
    pair_all = lax.all_gather(
        jnp.concatenate([key_rows, value_rows], axis=1), "ctx", axis=0, tiled=True
    )
    kv_width = key_rows.shape[1]
    keys_all, values_all = (pair_all[:, :kv_width], pair_all[:, kv_width:])
    tokens = keys_all.shape[0]
    block_rows = math.gcd(512, tokens)

    def fetch(table, block_number):
        return lax.dynamic_slice_in_dim(table, block_number * block_rows, block_rows, 0)

    def column_pos(block_number):
        return block_number * block_rows + jnp.arange(block_rows, dtype=jnp.int32)

    buffer = jnp.zeros((tokens, 2 * local_groups * head_dim), jnp.float32)
    rows = query_rows.shape[0]
    row_pos = first_row + jnp.arange(rows, dtype=jnp.int32)
    needed = (first_row + rows - 1) // block_rows + 1
    query_heads = query_rows.reshape(rows, local_groups, group_size, head_dim)
    log_totals = []
    shared_head = 0
    query_group = query_heads[:, shared_head]

    def stats_step(block_number, carried):
        running_max, running_sum = carried
        key_block = fetch(keys_all, block_number)
        scores = block_scores(query_group, key_block, scaling, row_pos, column_pos(block_number))
        new_max = jnp.maximum(running_max, jnp.max(scores, axis=-1))
        running_sum = running_sum * jnp.exp(running_max - new_max) + jnp.sum(
            jnp.exp(scores - new_max[..., None]), axis=-1
        )
        return (new_max, running_sum)

    start_max = jnp.full((rows, group_size), NEGATIVE, jnp.float32)
    start_sum = jnp.zeros((rows, group_size), jnp.float32)
    running_max, running_sum = lax.fori_loop(0, needed, stats_step, (start_max, start_sum))
    log_total = running_max + jnp.log(running_sum)

    def value_step(block_number, accumulated):
        key_block = fetch(keys_all, block_number)
        value_block = fetch(values_all, block_number)
        scores = block_scores(query_group, key_block, scaling, row_pos, column_pos(block_number))
        rounded = jnp.exp(scores - log_total[..., None]).astype(jnp.bfloat16)
        return accumulated + jnp.einsum(
            "tgk,kd->tgd", rounded, value_block, preferred_element_type=jnp.float32
        )

    accumulated = lax.fori_loop(
        0, needed, value_step, jnp.zeros((rows, group_size, head_dim), jnp.float32)
    )
    log_totals.append(log_total)
    attended_list = [accumulated.astype(jnp.bfloat16)]
    attended_part = jnp.stack(attended_list, axis=1).reshape(
        rows, local_groups * group_size * head_dim
    )
    log_totals, attended = (log_totals, attended_part)
    piece_part = lax.all_gather(weighted, "head", axis=1, tiled=True)
    grad_sum = lax.dot_general(
        piece_part, out_weight, (((1,), (1,)), ((), ())), preferred_element_type=jnp.float32
    )
    grad_sum, squares_out = (grad_sum, gram_squares(piece_part, attended, head_dim))
    grad_attended, squares_out = (grad_sum.astype(jnp.bfloat16), squares_out)
    backward_buffer = buffer
    rows = query_rows.shape[0]
    backward_row_pos = first_row + jnp.arange(rows, dtype=jnp.int32)
    needed = (first_row + rows - 1) // block_rows + 1
    query_heads = query_rows.reshape(rows, local_groups, group_size, head_dim)
    grad_heads = grad_attended.reshape(rows, local_groups, group_size, head_dim)
    attended_heads = attended.reshape(rows, local_groups, group_size, head_dim)
    shared_head = 0
    backward_query_group = query_heads[:, shared_head]
    grad_group = grad_heads[:, shared_head]
    backward_log_total = log_totals[shared_head]
    row_dot = jnp.sum(
        grad_group.astype(jnp.float32) * attended_heads[:, shared_head].astype(jnp.float32), axis=-1
    )
    key_column = jnp.int32(shared_head * head_dim)
    value_column = jnp.int32((local_groups + shared_head) * head_dim)

    def back_step(block_number, carried):
        query_sum, buffer_now = carried
        key_block = fetch(keys_all, block_number)
        value_block = fetch(values_all, block_number)
        scores = block_scores(
            backward_query_group, key_block, scaling, backward_row_pos, column_pos(block_number)
        )
        softmax = jnp.exp(scores - backward_log_total[..., None])
        rounded = softmax.astype(jnp.bfloat16)
        grad_prob = jnp.einsum(
            "tgd,kd->tgk", grad_group, value_block, preferred_element_type=jnp.float32
        )
        grad_score = (softmax * (grad_prob - row_dot[..., None]) * scaling).astype(jnp.bfloat16)
        query_sum = query_sum + jnp.einsum(
            "tgk,kd->tgd", grad_score, key_block, preferred_element_type=jnp.float32
        )
        key_part = jnp.einsum(
            "tgk,tgd->kd", grad_score, backward_query_group, preferred_element_type=jnp.float32
        )
        value_part = jnp.einsum(
            "tgk,tgd->kd", rounded, grad_group, preferred_element_type=jnp.float32
        )
        row_start = (block_number * block_rows).astype(jnp.int32)
        old_key = lax.dynamic_slice(buffer_now, (row_start, key_column), (block_rows, head_dim))
        buffer_now = lax.dynamic_update_slice(
            buffer_now, old_key + key_part, (row_start, key_column)
        )
        old_value = lax.dynamic_slice(buffer_now, (row_start, value_column), (block_rows, head_dim))
        buffer_now = lax.dynamic_update_slice(
            buffer_now, old_value + value_part, (row_start, value_column)
        )
        return (query_sum, buffer_now)

    start_query = jnp.zeros((rows, group_size, head_dim), jnp.float32)
    query_sum, backward_buffer = lax.fori_loop(0, needed, back_step, (start_query, backward_buffer))
    query_grads = [query_sum.astype(jnp.bfloat16)]
    grad_query_part = jnp.stack(query_grads, axis=1).reshape(
        rows, local_groups * group_size * head_dim
    )
    key_sums = lax.psum_scatter(
        backward_buffer.astype(jnp.bfloat16), "ctx", scatter_dimension=0, tiled=True
    ).astype(jnp.float32)
    grad_key = key_sums[:, : local_groups * head_dim].astype(jnp.bfloat16)
    grad_value = key_sums[:, local_groups * head_dim :].astype(jnp.bfloat16)
    squares_query = gram_pair_squares(hidden_gram, grad_query_part, head_dim)
    normal_size = D * head_dim * tok_dev
    fisher_q = jnp.log(squares_query / normal_size + EPSILON).reshape(1, -1)
    fisher_o = jnp.log(squares_out / normal_size + EPSILON).reshape(1, -1)
    return (grad_query_part, grad_key, grad_value, fisher_q, fisher_o)


def solution(mesh):
    return jax.shard_map(
        body,
        mesh=mesh,
        in_specs=(
            P("ctx", "head"),
            P("ctx", "head"),
            P("ctx", "head"),
            P("ctx", "head"),
            P("head", None),
            P("ctx", "head"),
            P("ctx"),
        ),
        out_specs=(
            P("ctx", "head"),
            P("ctx", "head"),
            P("ctx", "head"),
            P("ctx", "head"),
            P("ctx", "head"),
        ),
        check_vma=False,
    )
```

profile of v0, /device:TPU:0, one launch (start us, length us, event | category | flops | bytes accessed | tf_op | source)
XLA Modules:
  0.0 287.8 jit_solution(4906694200121494240)
XLA Ops:
  7.2 0.0 copy-start
  7.2 0.0 all-gather.3.cloned.1.call-start
  7.2 1.6 pad_maximum_fusion
  8.8 0.0 all-gather.3.cloned.1.call-update
  8.8 0.0 all-gather.5.cloned.1.call-start
  8.9 0.7 convert_add_fusion
  9.6 2.0 multiply_convert_fusion
  11.6 0.0 all-gather.5.cloned.1.call-update
  11.6 0.0 all-reduce.2.cloned.1.call-start
  11.6 0.0 copy-done
  11.6 1.0 fusion.64
  12.7 0.0 all-reduce.2.cloned.1.call-update
  12.7 0.0 reduce-scatter.2.cloned.1.call-start
  12.8 1.2 copy.18
  14.0 0.3 copy.22
  14.3 1.1 copy.21
  15.4 31.1 %all-gather.3.cloned.1.call-done = bf16[4096,256]{1,0:T(8,128)(2,1)} async-done(((bf16[256,256]{1,0:T(8,128)(2,1)}), bf16[4096,256]{1,0:T(8,128)(2,1)}) %all-gather.3.cloned.1.call-update) | async-done | bytes 2097168 | tf_op jit(solution)/shard_map/all_gather | solution.py:65
  46.4 2.7 fusion.62
  49.2 1.9 while.37
  49.2 0.1 broadcast_compare_fusion.6
  49.3 0.8 fusion.100
  50.1 0.9 exponential_reduce_fusion.2
  51.1 0.1 broadcast.137.clone
  51.1 3.0 %while.38 = (s32[]{:T(128)}, f32[256,8,128]{2,0,1:T(8,128)S(1)}, s32[]{:T(128)}, bf16[4096,128]{1,0:T(8,128)(2,1)S(1)}, bf16[256,8,128]{2,1,0:T(8,128)(2,1)}, /*...) while((s32[]{:T(128)}, f32[256,8,128]{2,0,1:T(8,128)S(1)}, ...), condition=%wide.region_5.6_spmd.clone, body=%wide.region_4.5_spmd.clone.sunk | while | flops 541459200 | bytes 3161259 | solution.py:112
  51.2 0.1 broadcast_compare_fusion.7
  51.3 2.8 fusion.104
  54.1 0.0 copy-start.1
  54.1 65.9 %all-gather.5.cloned.1.call-done = bf16[256,8192]{1,0:T(8,128)(2,1)} async-done(((bf16[256,1024]{1,0:T(8,128)(2,1)}), bf16[256,8192]{1,0:T(8,128)(2,1)}) %all-gather.5.cloned.1.call-update) | async-done | bytes 4194320 | tf_op jit(solution)/shard_map/all_gather | solution.py:121
  120.1 12.4 %fusion.59 = bf16[32,8,8,128]{3,2,1,0:T(8,128)(2,1)} fusion(bf16[256,8192]{1,0:T(8,128)(2,1)} %all-gather.5.cloned.1.call-done, bf16[1024,8192]{1,0:T(8,128)(2,1)} %param.17), kind=kOutput, calls=%fused_computation.65 | convolution fusion | flops 4295229440 | bytes 21495808 | tf_op jit(solution)/shard_map/dot_general | solution.py:122
  132.4 1.9 copy.36
  134.4 0.0 copy-done.1
  134.4 1.4 multiply_reduce_fusion.2
  135.8 0.1 broadcast.137
  135.8 2.2 broadcast_in_dim.50
  138.1 9.5 %while.39 = (s32[]{:T(128)}, f32[256,8,128]{2,0,1:T(8,128)S(1)}, f32[4096,256]{1,0:T(8,128)}, s32[]{:T(128)}, bf16[4096,128]{1,0:T(8,128)(2,1)S(1)}, /*index=5*/...) while((s32[]{:T(128)}, f32[256,8,128]{2,0,1:T(8,128)S(1)}, ...), condition=%wide.region_8.9_spmd.clone, body=%wide.region_7.8_spmd.clone.sunk | while | flops 1354236672 | bytes 27031796 | solution.py:178
  138.1 0.0 copy-start.3
  138.1 0.1 broadcast_compare_fusion.8
  138.2 0.7 fusion.115
  139.0 0.2 copy-done.3
  139.1 2.4 fusion.116
  141.5 0.9 convolution_add_fusion.2
  142.5 2.4 fusion.117
  144.9 2.7 fusion.118
  147.6 3.8 %convert_element_type.47 = bf16[4096,256]{1,0:T(8,128)(2,1)} convert(f32[4096,256]{1,0:T(8,128)} %get-tuple-element.150) | non-fusion elementwise | flops 1048576 | bytes 6291456 | tf_op jit(solution)/shard_map/convert_element_type | solution.py:184
  151.4 0.0 reduce-scatter.2.cloned.1.call-update
  151.4 0.0 copy-start.2
  151.4 4.8 %fusion.65 = f32[256,256]{1,0:T(8,128)S(1)} fusion(bf16[256,8192]{1,0:T(8,128)(2,1)} %all-gather.5.cloned.1.call-done), kind=kOutput, calls=%fused_computation.81 | convolution fusion | flops 1073741824 | bytes 4456448 | tf_op jit(solution)/shard_map/dot_general | solution.py:43
  156.2 0.0 copy-done.2
  156.3 0.5 multiply_reduce_fusion
  156.8 47.9 %all-reduce.2.cloned.1.call-done = f32[256,256]{1,0:T(8,128)} async-done(((f32[256,256]{1,0:T(8,128)}), f32[256,256]{1,0:T(8,128)}) %all-reduce.2.cloned.1.call-update) | async-done | bytes 262160 | tf_op jit(solution)/shard_map/psum | solution.py:59
  204.7 1.5 multiply_reduce_fusion.1
  206.2 0.5 log_bitcast_fusion
  206.7 0.5 log_bitcast_fusion.1
  207.2 0.9 copy_bitcast_fusion
  208.1 71.6 %reduce-scatter.2.cloned.1.call-done = bf16[256,256]{1,0:T(8,128)(2,1)} async-done(((bf16[4096,256]{1,0:T(8,128)(2,1)}), bf16[256,256]{1,0:T(8,128)(2,1)}) %reduce-scatter.2.cloned.1.call-update) | async-done | bytes 131088 | tf_op jit(solution)/shard_map/reduce_scatter | solution.py:183
  279.7 1.5 fusion.63
  (12 shorter events, 0.0 us)
Async XLA Ops:
  7.2 4.5 %copy-start = (bf16[256,1024]{1,0:T(8,128)(2,1)S(1)}, bf16[256,1024]{1,0:T(8,128)(2,1)}, u32[]{:S(2)}) copy-start(bf16[256,1024]{1,0:T(8,128)(2,1)} %param.13) | copy-start | bytes 1572868
  7.2 39.3 %all-gather.3.cloned.1.call-start = ((), (), s32[]{:S(2)}) async-start(), calls=%async_computation.1 | async-start | bytes 2228224 | tf_op jit(solution)/shard_map/all_gather | solution.py:65
  8.8 111.3 %all-gather.5.cloned.1.call-start = ((), (), s32[]{:S(2)}) async-start(), calls=%async_computation.2 | async-start | bytes 4718592 | tf_op jit(solution)/shard_map/all_gather | solution.py:121
  11.6 193.1 %all-reduce.2.cloned.1.call-start = ((), (), s32[]{:S(2)}) async-start(), calls=%async_computation.4 | async-start | bytes 524288 | tf_op jit(solution)/shard_map/psum | solution.py:59
  12.7 267.0 %reduce-scatter.2.cloned.1.call-start = ((), (), s32[]{:S(2)}) async-start(), calls=%async_computation.3 | async-start | bytes 2228224 | tf_op jit(solution)/shard_map/reduce_scatter | solution.py:183
  54.1 80.2 %copy-start.1 = (f32[256,8,128]{2,0,1:T(8,128)}, f32[256,8,128]{2,0,1:T(8,128)S(1)}, u32[]{:S(2)}) copy-start(f32[256,8,128]{2,0,1:T(8,128)S(1)} %get-tuple-element.148) | copy-start | bytes 3145732
  138.1 1.0 copy-start.3
  151.4 4.8 %copy-start.2 = (f32[256,8,128]{2,0,1:T(8,128)S(1)}, f32[256,8,128]{2,0,1:T(8,128)}, u32[]{:S(2)}) copy-start(f32[256,8,128]{2,0,1:T(8,128)} %copy-done.1) | copy-start | bytes 3145732
Sparse Core Ops, SparseCore 0:
  9.7 36.6 all-gather.2
  48.8 71.2 all-gather.4
  122.6 82.0 all-reduce.1
  207.1 72.5 reduce-scatter.1
where the time goes:
time: 289 us; the launch traced here: 288 us
  waiting for transfers between devices  217 us (75%)
  matrix products  33 us (11%)
  between operations  13.9 us (5%)
  other arithmetic  12.7 us (4%)
  local copies, waits for them, and re-layouts  11.4 us (4%)
    reduce_scatter x1, waiting for transfers between devices, body(): lax.psum_scatter(backward_buffer.astype(jnp.bfloat16), 'ctx', scatter_dim...  71.6 us
    all_gather x1, waiting for transfers between devices, body(): piece_part = lax.all_gather(weighted, 'head', axis=1, tiled=True)  65.9 us
    psum x1, waiting for transfers between devices, body(): lax.psum(lax.dot_general(hidden_in, hidden_in, (((1,), (1,)), ((), ())),...  47.9 us
    all_gather x1, waiting for transfers between devices, body(): lax.all_gather(jnp.concatenate([key_rows, value_rows], axis=1), 'ctx', ax...  31.1 us
    dot_general x1, matrix products, body(): lax.dot_general(piece_part, out_weight, (((1,), (1,)), ((), ())), preferr...  12.4 us
  transfers between devices with their start and end apart: 4, of which 4 were waited for; matrix products, arithmetic and copies ran while one was open for 19% of the time, Pallas kernels for 0%

commit v1 on v0

--- a/solution.py
+++ b/solution.py
@@ -56,11 +56,14 @@
     first_row = own_index * tok_dev
     loss_weight = 0.25 + answer_mask.astype(jnp.float32)
     weighted = (grad_out.astype(jnp.float32) * loss_weight[:, None]).astype(jnp.bfloat16)
-    hidden_gram = lax.psum(
-        lax.dot_general(
-            hidden_in, hidden_in, (((1,), (1,)), ((), ())), preferred_element_type=jnp.float32
+    hidden_gram = jnp.sum(
+        lax.all_gather(
+            lax.dot_general(
+                hidden_in, hidden_in, (((1,), (1,)), ((), ())), preferred_element_type=jnp.float32
+            ),
+            "head",
         ),
-        "head",
+        axis=0,
     )
     pair_all = lax.all_gather(
         jnp.concatenate([key_rows, value_rows], axis=1), "ctx", axis=0, tiled=True

time: 289 us -> 289 us (level)
    psum x1 -> x0, waiting for transfers between devices: 47.9 us -> none  [body(): lax.psum(lax.dot_general(hidden_in, hidden_in, (((1,), (1,)), ((), ())),...]
    all_gather x0 -> x1, waiting for transfers between devices: none -> 24 us  [body(): lax.all_gather(lax.dot_general(hidden_in, hidden_in, (((1,), (1,)), ((),...]
    reduce_scatter x1, waiting for transfers between devices: 71.6 us -> 95.3 us  [body(): lax.psum_scatter(backward_buffer.astype(jnp.bfloat16), 'ctx', scatter_dim...]
where the time goes in v1:
time: 289 us; the launch traced here: 288 us
  waiting for transfers between devices  216 us (75%)
  matrix products  32 us (11%)
  between operations  13.9 us (5%)
  other arithmetic  13.8 us (5%)
  local copies, waits for them, and re-layouts  11.3 us (4%)
    reduce_scatter x1, waiting for transfers between devices, body(): lax.psum_scatter(backward_buffer.astype(jnp.bfloat16), 'ctx', scatter_dim...  95.3 us
    all_gather x1, waiting for transfers between devices, body(): piece_part = lax.all_gather(weighted, 'head', axis=1, tiled=True)  66 us
    all_gather x1, waiting for transfers between devices, body(): lax.all_gather(jnp.concatenate([key_rows, value_rows], axis=1), 'ctx', ax...  31.1 us
    all_gather x1, waiting for transfers between devices, body(): lax.all_gather(lax.dot_general(hidden_in, hidden_in, (((1,), (1,)), ((),...  24 us
    dot_general x1, matrix products, body(): lax.dot_general(piece_part, out_weight, (((1,), (1,)), ((), ())), preferr...  12.4 us
  transfers between devices with their start and end apart: 4, of which 4 were waited for; matrix products, arithmetic and copies ran while one was open for 19% of the time, Pallas kernels for 0%

profile of v1, /device:TPU:0, one launch (start us, length us, event | category | flops | bytes accessed | tf_op | source)
XLA Modules:
  0.0 287.8 jit_solution(17035835455614103852)
XLA Ops:
  7.2 0.0 copy-start
  7.2 0.0 all-gather.5.cloned.1.call-start
  7.2 1.6 pad_maximum_fusion
  8.8 0.0 all-gather.5.cloned.1.call-update
  8.9 0.0 all-gather.7.cloned.1.call-start
  8.9 0.7 convert_add_fusion
  9.6 2.0 multiply_convert_fusion
  11.6 0.0 all-gather.7.cloned.1.call-update
  11.6 0.0 all-gather.9.cloned.1.call-start
  11.7 0.0 copy-done
  11.7 1.0 fusion.64
  12.7 0.0 all-gather.9.cloned.1.call-update
  12.7 0.0 reduce-scatter.2.cloned.1.call-start
  12.8 1.2 copy.18
  14.0 0.3 copy.22
  14.3 1.1 copy.21
  15.4 31.1 %all-gather.5.cloned.1.call-done = bf16[4096,256]{1,0:T(8,128)(2,1)} async-done(((bf16[256,256]{1,0:T(8,128)(2,1)}), bf16[4096,256]{1,0:T(8,128)(2,1)}) %all-gather.5.cloned.1.call-update) | async-done | bytes 2097168 | tf_op jit(solution)/shard_map/all_gather | solution.py:68
  46.4 2.6 fusion.62
  49.1 1.9 while.37
  49.1 0.1 broadcast_compare_fusion.6
  49.3 0.8 fusion.100
  50.1 0.9 exponential_reduce_fusion.2
  51.0 0.1 broadcast.137.clone
  51.1 3.0 %while.38 = (s32[]{:T(128)}, f32[256,8,128]{2,0,1:T(8,128)S(1)}, s32[]{:T(128)}, bf16[4096,128]{1,0:T(8,128)(2,1)S(1)}, bf16[256,8,128]{2,1,0:T(8,128)(2,1)}, /*...) while((s32[]{:T(128)}, f32[256,8,128]{2,0,1:T(8,128)S(1)}, ...), condition=%wide.region_5.6_spmd.clone, body=%wide.region_4.5_spmd.clone.sunk | while | flops 541459200 | bytes 3161259 | solution.py:115
  51.1 0.1 broadcast_compare_fusion.7
  51.3 2.8 fusion.104
  54.1 0.0 copy-start.1
  54.1 66.0 %all-gather.7.cloned.1.call-done = bf16[256,8192]{1,0:T(8,128)(2,1)} async-done(((bf16[256,1024]{1,0:T(8,128)(2,1)}), bf16[256,8192]{1,0:T(8,128)(2,1)}) %all-gather.7.cloned.1.call-update) | async-done | bytes 4194320 | tf_op jit(solution)/shard_map/all_gather | solution.py:124
  120.1 12.4 %fusion.59 = bf16[32,8,8,128]{3,2,1,0:T(8,128)(2,1)} fusion(bf16[256,8192]{1,0:T(8,128)(2,1)} %all-gather.7.cloned.1.call-done, bf16[1024,8192]{1,0:T(8,128)(2,1)} %param.17), kind=kOutput, calls=%fused_computation.65 | convolution fusion | flops 4295229440 | bytes 21495808 | tf_op jit(solution)/shard_map/dot_general | solution.py:125
  132.5 1.9 copy.36
  134.4 0.0 copy-done.1
  134.4 1.4 multiply_reduce_fusion.2
  135.8 0.1 broadcast.137
  135.8 2.2 broadcast_in_dim.50
  138.1 9.5 %while.39 = (s32[]{:T(128)}, f32[256,8,128]{2,0,1:T(8,128)S(1)}, f32[4096,256]{1,0:T(8,128)}, s32[]{:T(128)}, bf16[4096,128]{1,0:T(8,128)(2,1)S(1)}, /*index=5*/...) while((s32[]{:T(128)}, f32[256,8,128]{2,0,1:T(8,128)S(1)}, ...), condition=%wide.region_8.9_spmd.clone, body=%wide.region_7.8_spmd.clone.sunk | while | flops 1354236672 | bytes 27031796 | solution.py:181
  138.1 0.0 copy-start.3
  138.1 0.1 broadcast_compare_fusion.8
  138.3 0.7 fusion.115
  139.0 0.2 copy-done.3
  139.1 2.4 fusion.116
  141.6 0.9 convolution_add_fusion.2
  142.5 2.4 fusion.117
  144.9 2.7 fusion.118
  147.6 3.7 %convert_element_type.47 = bf16[4096,256]{1,0:T(8,128)(2,1)} convert(f32[4096,256]{1,0:T(8,128)} %get-tuple-element.150) | non-fusion elementwise | flops 1048576 | bytes 6291456 | tf_op jit(solution)/shard_map/convert_element_type | solution.py:187
  151.3 0.0 reduce-scatter.2.cloned.1.call-update
  151.3 24.0 %all-gather.9.cloned.1.call-done = f32[2048,256]{1,0:T(8,128)} async-done(((f32[256,256]{1,0:T(8,128)}), f32[2048,256]{1,0:T(8,128)}) %all-gather.9.cloned.1.call-update) | async-done | bytes 2097168 | tf_op jit(solution)/shard_map/all_gather | solution.py:60
  175.3 1.8 reduce_sum.46
  177.0 0.0 copy-start.2
  177.1 4.8 %fusion.65 = f32[256,256]{1,0:T(8,128)S(1)} fusion(bf16[256,8192]{1,0:T(8,128)(2,1)} %all-gather.7.cloned.1.call-done), kind=kOutput, calls=%fused_computation.81 | convolution fusion | flops 1073741824 | bytes 4456448 | tf_op jit(solution)/shard_map/dot_general | solution.py:43
  181.9 0.0 copy-done.2
  181.9 0.5 multiply_reduce_fusion
  182.4 0.5 multiply_reduce_fusion.1
  183.0 0.5 log_bitcast_fusion
  183.5 0.9 copy_bitcast_fusion
  184.4 95.3 %reduce-scatter.2.cloned.1.call-done = bf16[256,256]{1,0:T(8,128)(2,1)} async-done(((bf16[4096,256]{1,0:T(8,128)(2,1)}), bf16[256,256]{1,0:T(8,128)(2,1)}) %reduce-scatter.2.cloned.1.call-update) | async-done | bytes 131088 | tf_op jit(solution)/shard_map/reduce_scatter | solution.py:186
  279.7 1.5 fusion.63
  (12 shorter events, 0.0 us)
Async XLA Ops:
  7.2 4.5 %copy-start = (bf16[256,1024]{1,0:T(8,128)(2,1)S(1)}, bf16[256,1024]{1,0:T(8,128)(2,1)}, u32[]{:S(2)}) copy-start(bf16[256,1024]{1,0:T(8,128)(2,1)} %param.13) | copy-start | bytes 1572868
  7.2 39.3 %all-gather.5.cloned.1.call-start = ((), (), s32[]{:S(2)}) async-start(), calls=%async_computation.1 | async-start | bytes 2228224 | tf_op jit(solution)/shard_map/all_gather | solution.py:68
  8.9 111.2 %all-gather.7.cloned.1.call-start = ((), (), s32[]{:S(2)}) async-start(), calls=%async_computation.2 | async-start | bytes 4718592 | tf_op jit(solution)/shard_map/all_gather | solution.py:124
  11.6 163.7 %all-gather.9.cloned.1.call-start = ((), (), s32[]{:S(2)}) async-start(), calls=%async_computation.4 | async-start | bytes 2359296 | tf_op jit(solution)/shard_map/all_gather | solution.py:60
  12.7 267.0 %reduce-scatter.2.cloned.1.call-start = ((), (), s32[]{:S(2)}) async-start(), calls=%async_computation.3 | async-start | bytes 2228224 | tf_op jit(solution)/shard_map/reduce_scatter | solution.py:186
  54.1 80.3 %copy-start.1 = (f32[256,8,128]{2,0,1:T(8,128)}, f32[256,8,128]{2,0,1:T(8,128)S(1)}, u32[]{:S(2)}) copy-start(f32[256,8,128]{2,0,1:T(8,128)S(1)} %get-tuple-element.148) | copy-start | bytes 3145732
  138.1 1.1 copy-start.3
  177.0 4.8 %copy-start.2 = (f32[256,8,128]{2,0,1:T(8,128)S(1)}, f32[256,8,128]{2,0,1:T(8,128)}, u32[]{:S(2)}) copy-start(f32[256,8,128]{2,0,1:T(8,128)} %copy-done.1) | copy-start | bytes 3145732
Sparse Core Ops, SparseCore 0:
  9.7 36.6 all-gather.4
  48.8 71.2 all-gather.6
  122.4 52.8 all-gather.8
  177.5 102.1 reduce-scatter.1
